TPU v7x, 512 devices: a whole 4x8x8 slice. The times are simulated.
512 devices in a mesh: sep: 8 (over y), row: 8 (over z), col: 8 (over x, core).
Axes of the slice: x: 4, y: 8, z: 8, core: 2. Of those that a mesh axis runs over, the one named last changes fastest.
Arguments:
- right_sides: float32 [2, 16, 32768], P(None, None, ('sep', 'row', 'col')), may hold values from -6 to 6
- inverse_diag: float32 [8, 4096, 4096], P('sep', ('row', 'col')), may hold values from -0.09375 to 0.09375
- lower_blocks: float32 [8, 2048, 4096], P('sep', ('row', 'col')), may hold values from -0.09375 to 0.09375
- targets: int32 [8, 2048], P('sep', ('row', 'col')), may hold values from 0 to 32767, as said below
- counts: int32 [8, 64], P('sep', ('row', 'col')), may hold values from 0 to 32, as said below
Outputs:
- solution: float32 [2, 16, 32768], P(None, None, ('sep', 'row', 'col'))
Inputs may be any that keep to these rules, and one draw needn't show every extreme that they name: For every separator s and lower row j: targets[s, j] // 4096 > s, except for the last separator whose counts are all zero; and (targets[s, j] % 4096) // 64 == j // 32. The last separator's counts are zero; every other separator has a block with exactly 32 live rows, and the others at least one.
All inputs are finite; a program needn't handle non-finite values.
Results may differ from a plain program's by a relative error of at most 0.0001.
Values sent between devices are 32-bit elements; how exact they have to be, the bound alone decides.
No kernel may reach another device: no remote copies, remote signals or barrier semaphores. Data moves between devices by JAX's collectives and lax.ppermute only.
A program may use at most 64 MiB of HBM per device.

v0:
```python
import jax
import jax.numpy as jnp
from jax import lax
from jax.sharding import PartitionSpec as P


def passed_along(block, axis, distance):
    devices = range(lax.axis_size(axis))
    route = [(i - distance, i) for i in devices if i - distance in devices]
    return lax.ppermute(block, axis, route)


def shards(right_sides, inverse_diag, lower_blocks, targets, counts):
    levels = lax.axis_size("sep")
    own_level = lax.axis_index("sep")
    batches, width_rhs, own_rows = right_sides.shape
    width = inverse_diag.shape[-1]
    given = right_sides.reshape(batches * width_rhs, own_rows)
    diag_rows = inverse_diag[0]
    lower_rows = lower_blocks[0]
    lower_count = lower_rows.shape[0]
    live = jnp.arange(lower_count, dtype=jnp.int32) < counts[0, 0]
    places = targets[0] // width * own_rows + targets[0] % own_rows

    def solve_piece(segment):
        return lax.dot_general(
            segment,
            diag_rows,
            (((1,), (1,)), ((), ())),
            precision=lax.Precision.HIGHEST,
            preferred_element_type=jnp.float32,
        )

    def lower_piece(segment):
        return lax.dot_general(
            segment,
            lower_rows,
            (((1,), (1,)), ((), ())),
            precision=lax.Precision.HIGHEST,
            preferred_element_type=jnp.float32,
        )

    def one_level(level, state):
        carried, solution = state
        resid = given - lax.dynamic_slice_in_dim(carried, level * own_rows, own_rows, 1)
        solved = solve_piece(lax.all_gather(resid, ("row", "col"), axis=1, tiled=True))
        solution = jnp.where(own_level == level, solved, solution)
        update = lower_piece(lax.all_gather(solved, ("row", "col"), axis=1, tiled=True))
        update = jnp.where(live[None, :], update, jnp.float32(0.0))
        carried = carried.at[:, places].add(update)
        return (passed_along(carried, "sep", 1), solution)

    carried = jnp.zeros((given.shape[0], levels * own_rows), jnp.float32)
    solution = jnp.zeros_like(given)
    carried, solution = lax.fori_loop(0, levels - 1, one_level, (carried, solution))
    last = levels - 1
    resid = given - carried[:, last * own_rows :]
    solved = solve_piece(lax.all_gather(resid, ("row", "col"), axis=1, tiled=True))
    solution = jnp.where(own_level == last, solved, solution)
    return solution.reshape(batches, width_rhs, own_rows)


def solution(mesh):
    placed = (
        P(None, None, ("sep", "row", "col")),
        P("sep", ("row", "col"), None),
        P("sep", ("row", "col"), None),
        P("sep", ("row", "col")),
        P("sep", ("row", "col")),
    )
    return jax.shard_map(
        shards,
        mesh=mesh,
        in_specs=placed,
        out_specs=P(None, None, ("sep", "row", "col")),
        check_vma=False,
    )
```

profile of v0, /device:TPU:33, one launch (start us, length us, event | category | flops | bytes accessed | tf_op | source)
XLA Modules:
  0.0 871.5 jit_solution(13566988338382411557)
XLA Ops:
  1.5 816.8 %while.16 = (s32[]{:T(128)}, f32[32,512]{0,1:T(8,128)S(1)}, f32[32,64]{1,0:T(8,128)S(1)}, s32[32]{0:T(128)S(1)}, f32[32,64]{0,1:T(8,128)S(1)}, /*index=5*/f32[64...) while((s32[]{:T(128)}, f32[32,512]{0,1:T(8,128)S(1)}, ...), condition=%wide.region_2.3_spmd.clone, body=%wide.region_0.2_spmd.clone.sunk | while | flops 151003264 | bytes 14787303 | solution.py:55
  1.8 57.0 %all-gather.7 = f32[64,64,32]{1,2,0:T(8,128)S(1)} all-gather(f32[1,64,32]{1,2,0:T(8,128)S(1)} %subtract_bitcast_fusion.2), channel_id=1, replica_groups=mesh['sep'=8,'row'=8,'col'=8] {'row','col'}, dimensions={0}, use_global_device_ids=true | all-gather | bytes 532480 | tf_op jit(solution)/shard_map/while/body/eval_jaxpr/all_gather | solution.py:46
  61.6 49.6 %all-gather.8 = f32[64,64,32]{1,2,0:T(8,128)S(1)} all-gather(f32[1,64,32]{1,2,0:T(8,128)S(1)} %bitcast.68), channel_id=1, replica_groups=mesh['sep'=8,'row'=8,'col'=8] {'row','col'}, dimensions={0}, use_global_device_ids=true | all-gather | bytes 532480 | tf_op jit(solution)/shard_map/while/body/eval_jaxpr/all_gather | solution.py:48
  114.4 2.3 collective-permute-start
  116.7 8.5 collective-permute-done
  125.5 48.8 %all-gather.7 = f32[64,64,32]{1,2,0:T(8,128)S(1)} all-gather(f32[1,64,32]{1,2,0:T(8,128)S(1)} %subtract_bitcast_fusion.2), channel_id=1, replica_groups=mesh['sep'=8,'row'=8,'col'=8] {'row','col'}, dimensions={0}, use_global_device_ids=true | all-gather | bytes 532480 | tf_op jit(solution)/shard_map/while/body/eval_jaxpr/all_gather | solution.py:46
  177.1 49.6 %all-gather.8 = f32[64,64,32]{1,2,0:T(8,128)S(1)} all-gather(f32[1,64,32]{1,2,0:T(8,128)S(1)} %bitcast.68), channel_id=1, replica_groups=mesh['sep'=8,'row'=8,'col'=8] {'row','col'}, dimensions={0}, use_global_device_ids=true | all-gather | bytes 532480 | tf_op jit(solution)/shard_map/while/body/eval_jaxpr/all_gather | solution.py:48
  231.8 8.9 %collective-permute-done = f32[32,512]{0,1:T(8,128)S(1)} collective-permute-done((f32[32,512]{0,1:T(8,128)S(1)}, f32[32,512]{0,1:T(8,128)S(1)}, u32[]{:S(2)}, u32[]{:S(2)}) %collective-permute-start) | collective-permute-done | bytes 65568 | tf_op jit(solution)/shard_map/while/body/eval_jaxpr/ppermute | solution.py:10
  241.0 48.8 %all-gather.7 = f32[64,64,32]{1,2,0:T(8,128)S(1)} all-gather(f32[1,64,32]{1,2,0:T(8,128)S(1)} %subtract_bitcast_fusion.2), channel_id=1, replica_groups=mesh['sep'=8,'row'=8,'col'=8] {'row','col'}, dimensions={0}, use_global_device_ids=true | all-gather | bytes 532480 | tf_op jit(solution)/shard_map/while/body/eval_jaxpr/all_gather | solution.py:46
  292.6 49.6 %all-gather.8 = f32[64,64,32]{1,2,0:T(8,128)S(1)} all-gather(f32[1,64,32]{1,2,0:T(8,128)S(1)} %bitcast.68), channel_id=1, replica_groups=mesh['sep'=8,'row'=8,'col'=8] {'row','col'}, dimensions={0}, use_global_device_ids=true | all-gather | bytes 532480 | tf_op jit(solution)/shard_map/while/body/eval_jaxpr/all_gather | solution.py:48
  347.3 8.9 %collective-permute-done = f32[32,512]{0,1:T(8,128)S(1)} collective-permute-done((f32[32,512]{0,1:T(8,128)S(1)}, f32[32,512]{0,1:T(8,128)S(1)}, u32[]{:S(2)}, u32[]{:S(2)}) %collective-permute-start) | collective-permute-done | bytes 65568 | tf_op jit(solution)/shard_map/while/body/eval_jaxpr/ppermute | solution.py:10
  356.5 48.8 %all-gather.7 = f32[64,64,32]{1,2,0:T(8,128)S(1)} all-gather(f32[1,64,32]{1,2,0:T(8,128)S(1)} %subtract_bitcast_fusion.2), channel_id=1, replica_groups=mesh['sep'=8,'row'=8,'col'=8] {'row','col'}, dimensions={0}, use_global_device_ids=true | all-gather | bytes 532480 | tf_op jit(solution)/shard_map/while/body/eval_jaxpr/all_gather | solution.py:46
  408.2 49.6 %all-gather.8 = f32[64,64,32]{1,2,0:T(8,128)S(1)} all-gather(f32[1,64,32]{1,2,0:T(8,128)S(1)} %bitcast.68), channel_id=1, replica_groups=mesh['sep'=8,'row'=8,'col'=8] {'row','col'}, dimensions={0}, use_global_device_ids=true | all-gather | bytes 532480 | tf_op jit(solution)/shard_map/while/body/eval_jaxpr/all_gather | solution.py:48
  462.9 8.9 %collective-permute-done = f32[32,512]{0,1:T(8,128)S(1)} collective-permute-done((f32[32,512]{0,1:T(8,128)S(1)}, f32[32,512]{0,1:T(8,128)S(1)}, u32[]{:S(2)}, u32[]{:S(2)}) %collective-permute-start) | collective-permute-done | bytes 65568 | tf_op jit(solution)/shard_map/while/body/eval_jaxpr/ppermute | solution.py:10
  472.0 48.8 %all-gather.7 = f32[64,64,32]{1,2,0:T(8,128)S(1)} all-gather(f32[1,64,32]{1,2,0:T(8,128)S(1)} %subtract_bitcast_fusion.2), channel_id=1, replica_groups=mesh['sep'=8,'row'=8,'col'=8] {'row','col'}, dimensions={0}, use_global_device_ids=true | all-gather | bytes 532480 | tf_op jit(solution)/shard_map/while/body/eval_jaxpr/all_gather | solution.py:46
  523.7 49.6 %all-gather.8 = f32[64,64,32]{1,2,0:T(8,128)S(1)} all-gather(f32[1,64,32]{1,2,0:T(8,128)S(1)} %bitcast.68), channel_id=1, replica_groups=mesh['sep'=8,'row'=8,'col'=8] {'row','col'}, dimensions={0}, use_global_device_ids=true | all-gather | bytes 532480 | tf_op jit(solution)/shard_map/while/body/eval_jaxpr/all_gather | solution.py:48
  578.4 8.9 %collective-permute-done = f32[32,512]{0,1:T(8,128)S(1)} collective-permute-done((f32[32,512]{0,1:T(8,128)S(1)}, f32[32,512]{0,1:T(8,128)S(1)}, u32[]{:S(2)}, u32[]{:S(2)}) %collective-permute-start) | collective-permute-done | bytes 65568 | tf_op jit(solution)/shard_map/while/body/eval_jaxpr/ppermute | solution.py:10
  587.6 48.8 %all-gather.7 = f32[64,64,32]{1,2,0:T(8,128)S(1)} all-gather(f32[1,64,32]{1,2,0:T(8,128)S(1)} %subtract_bitcast_fusion.2), channel_id=1, replica_groups=mesh['sep'=8,'row'=8,'col'=8] {'row','col'}, dimensions={0}, use_global_device_ids=true | all-gather | bytes 532480 | tf_op jit(solution)/shard_map/while/body/eval_jaxpr/all_gather | solution.py:46
  639.2 49.6 %all-gather.8 = f32[64,64,32]{1,2,0:T(8,128)S(1)} all-gather(f32[1,64,32]{1,2,0:T(8,128)S(1)} %bitcast.68), channel_id=1, replica_groups=mesh['sep'=8,'row'=8,'col'=8] {'row','col'}, dimensions={0}, use_global_device_ids=true | all-gather | bytes 532480 | tf_op jit(solution)/shard_map/while/body/eval_jaxpr/all_gather | solution.py:48
  693.9 8.9 %collective-permute-done = f32[32,512]{0,1:T(8,128)S(1)} collective-permute-done((f32[32,512]{0,1:T(8,128)S(1)}, f32[32,512]{0,1:T(8,128)S(1)}, u32[]{:S(2)}, u32[]{:S(2)}) %collective-permute-start) | collective-permute-done | bytes 65568 | tf_op jit(solution)/shard_map/while/body/eval_jaxpr/ppermute | solution.py:10
  703.1 48.8 %all-gather.7 = f32[64,64,32]{1,2,0:T(8,128)S(1)} all-gather(f32[1,64,32]{1,2,0:T(8,128)S(1)} %subtract_bitcast_fusion.2), channel_id=1, replica_groups=mesh['sep'=8,'row'=8,'col'=8] {'row','col'}, dimensions={0}, use_global_device_ids=true | all-gather | bytes 532480 | tf_op jit(solution)/shard_map/while/body/eval_jaxpr/all_gather | solution.py:46
  754.7 49.6 %all-gather.8 = f32[64,64,32]{1,2,0:T(8,128)S(1)} all-gather(f32[1,64,32]{1,2,0:T(8,128)S(1)} %bitcast.68), channel_id=1, replica_groups=mesh['sep'=8,'row'=8,'col'=8] {'row','col'}, dimensions={0}, use_global_device_ids=true | all-gather | bytes 532480 | tf_op jit(solution)/shard_map/while/body/eval_jaxpr/all_gather | solution.py:48
  809.4 8.9 %collective-permute-done = f32[32,512]{0,1:T(8,128)S(1)} collective-permute-done((f32[32,512]{0,1:T(8,128)S(1)}, f32[32,512]{0,1:T(8,128)S(1)}, u32[]{:S(2)}, u32[]{:S(2)}) %collective-permute-start) | collective-permute-done | bytes 65568 | tf_op jit(solution)/shard_map/while/body/eval_jaxpr/ppermute | solution.py:10
  819.1 49.0 %all-gather.2 = f32[64,64,32]{1,2,0:T(8,128)S(1)} all-gather(f32[1,64,32]{1,2,0:T(8,128)S(1)} %fusion.4), channel_id=1, replica_groups=mesh['sep'=8,'row'=8,'col'=8] {'row','col'}, dimensions={0}, use_global_device_ids=true | all-gather | bytes 532480 | tf_op jit(solution)/shard_map/all_gather | solution.py:58
  (147 shorter events, 60.5 us)
Async XLA Ops:
  0.8 0.7 copy-start.4
  59.4 1.2 copy-start
  111.8 1.0 copy-start.2
  114.4 10.8 %collective-permute-start = (f32[32,512]{0,1:T(8,128)S(1)}, f32[32,512]{0,1:T(8,128)S(1)}, u32[]{:S(2)}, u32[]{:S(2)}) collective-permute-start(f32[32,512]{0,1:T(8,128)S(1)} %scatter_fusion), channel_id=1, source_target_pairs={{0,64},{64,128},{128,192},{192,256},{256,320},{320,384},{384,448},... | collective-permute-start | bytes 196616 | tf_op jit(solution)/shard_map/while/body/eval_jaxpr/ppermute | solution.py:10
  174.9 1.2 copy-start
  227.4 1.0 copy-start.2
  229.9 10.8 %collective-permute-start = (f32[32,512]{0,1:T(8,128)S(1)}, f32[32,512]{0,1:T(8,128)S(1)}, u32[]{:S(2)}, u32[]{:S(2)}) collective-permute-start(f32[32,512]{0,1:T(8,128)S(1)} %scatter_fusion), channel_id=1, source_target_pairs={{0,64},{64,128},{128,192},{192,256},{256,320},{320,384},{384,448},... | collective-permute-start | bytes 196616 | tf_op jit(solution)/shard_map/while/body/eval_jaxpr/ppermute | solution.py:10
  290.5 1.2 copy-start
  342.9 1.0 copy-start.2
  345.4 10.8 %collective-permute-start = (f32[32,512]{0,1:T(8,128)S(1)}, f32[32,512]{0,1:T(8,128)S(1)}, u32[]{:S(2)}, u32[]{:S(2)}) collective-permute-start(f32[32,512]{0,1:T(8,128)S(1)} %scatter_fusion), channel_id=1, source_target_pairs={{0,64},{64,128},{128,192},{192,256},{256,320},{320,384},{384,448},... | collective-permute-start | bytes 196616 | tf_op jit(solution)/shard_map/while/body/eval_jaxpr/ppermute | solution.py:10
  406.0 1.2 copy-start
  458.4 1.0 copy-start.2
  460.9 10.8 %collective-permute-start = (f32[32,512]{0,1:T(8,128)S(1)}, f32[32,512]{0,1:T(8,128)S(1)}, u32[]{:S(2)}, u32[]{:S(2)}) collective-permute-start(f32[32,512]{0,1:T(8,128)S(1)} %scatter_fusion), channel_id=1, source_target_pairs={{0,64},{64,128},{128,192},{192,256},{256,320},{320,384},{384,448},... | collective-permute-start | bytes 196616 | tf_op jit(solution)/shard_map/while/body/eval_jaxpr/ppermute | solution.py:10
  521.5 1.2 copy-start
  573.9 1.0 copy-start.2
  576.4 10.8 %collective-permute-start = (f32[32,512]{0,1:T(8,128)S(1)}, f32[32,512]{0,1:T(8,128)S(1)}, u32[]{:S(2)}, u32[]{:S(2)}) collective-permute-start(f32[32,512]{0,1:T(8,128)S(1)} %scatter_fusion), channel_id=1, source_target_pairs={{0,64},{64,128},{128,192},{192,256},{256,320},{320,384},{384,448},... | collective-permute-start | bytes 196616 | tf_op jit(solution)/shard_map/while/body/eval_jaxpr/ppermute | solution.py:10
  637.0 1.2 copy-start
  689.4 1.0 copy-start.2
  692.0 10.8 %collective-permute-start = (f32[32,512]{0,1:T(8,128)S(1)}, f32[32,512]{0,1:T(8,128)S(1)}, u32[]{:S(2)}, u32[]{:S(2)}) collective-permute-start(f32[32,512]{0,1:T(8,128)S(1)} %scatter_fusion), channel_id=1, source_target_pairs={{0,64},{64,128},{128,192},{192,256},{256,320},{320,384},{384,448},... | collective-permute-start | bytes 196616 | tf_op jit(solution)/shard_map/while/body/eval_jaxpr/ppermute | solution.py:10
  752.5 1.2 copy-start
  804.9 1.0 copy-start.2
  807.5 10.8 %collective-permute-start = (f32[32,512]{0,1:T(8,128)S(1)}, f32[32,512]{0,1:T(8,128)S(1)}, u32[]{:S(2)}, u32[]{:S(2)}) collective-permute-start(f32[32,512]{0,1:T(8,128)S(1)} %scatter_fusion), channel_id=1, source_target_pairs={{0,64},{64,128},{128,192},{192,256},{256,320},{320,384},{384,448},... | collective-permute-start | bytes 196616 | tf_op jit(solution)/shard_map/while/body/eval_jaxpr/ppermute | solution.py:10
  818.3 0.7 copy-start.3
  868.7 1.2 copy-start.1
where the time goes:
time: 873 us; the launch traced here: 872 us
  blocking collectives  746 us (85%)
  waiting for transfers between devices  61.8 us (7%)
  local copies, waits for them, and re-layouts  25.6 us (3%)
  starting transfers between devices  13.8 us (2%)
  matrix products  12.1 us (1%)
  other arithmetic  11.3 us (1%)
    all_gather x7, blocking collectives, one_level(): lax.all_gather(resid, ('row', 'col'), axis=1, tiled=True)  350 us
    all_gather x7, blocking collectives, one_level(): lax.all_gather(solved, ('row', 'col'), axis=1, tiled=True)  347 us
    ppermute x7, waiting for transfers between devices, passed_along(): return lax.ppermute(block, axis, route)  61.8 us
    all_gather x1, blocking collectives, shards(): lax.all_gather(resid, ('row', 'col'), axis=1, tiled=True)  49 us
  transfers between devices with their start and end apart: 7, of which 7 were waited for; matrix products, arithmetic and copies ran while one was open for 0% of the time, Pallas kernels for 0%

commit v1 on v0

--- a/solution.py
+++ b/solution.py
@@ -1,7 +1,21 @@
+import functools
 import jax
 import jax.numpy as jnp
 from jax import lax
 from jax.sharding import PartitionSpec as P
+
+
+def part_targets(sample, which_dim):
+    base_arr = jnp.concatenate(
+        lax.all_to_all(
+            jnp.stack([sample for _ in range(lax.axis_size(("row", "col")))]), ("row", "col"), 0, 0
+        ),
+        which_dim,
+    )
+    return base_arr
+
+
+meet_pipes = functools.partial(part_targets, which_dim=1)
 
 
 def passed_along(block, axis, distance):
@@ -45,7 +59,7 @@
         resid = given - lax.dynamic_slice_in_dim(carried, level * own_rows, own_rows, 1)
         solved = solve_piece(lax.all_gather(resid, ("row", "col"), axis=1, tiled=True))
         solution = jnp.where(own_level == level, solved, solution)
-        update = lower_piece(lax.all_gather(solved, ("row", "col"), axis=1, tiled=True))
+        update = lower_piece(meet_pipes(solved))
         update = jnp.where(live[None, :], update, jnp.float32(0.0))
         carried = carried.at[:, places].add(update)
         return (passed_along(carried, "sep", 1), solution)

time: 873 us -> 727 us (0.83)
  blocking collectives: 746 us -> 409 us
  waiting for transfers between devices: 61.8 us -> 179 us
  starting transfers between devices: 13.8 us -> 52.1 us
  local copies, waits for them, and re-layouts: 25.6 us -> 47.7 us
  other arithmetic: 11.3 us -> 24.3 us
    all_gather x7 -> x0, blocking collectives: 347 us -> none  [one_level(): lax.all_gather(solved, ('row', 'col'), axis=1, tiled=True)]
    all_to_all x0 -> x7, waiting for transfers between devices: none -> 119 us  [part_targets(): lax.all_to_all(jnp.stack([sample for _ in range(lax.axis_size(('row', 'co...]
    all_to_all x0 -> x7, starting transfers between devices: none -> 38.2 us  [part_targets(): lax.all_to_all(jnp.stack([sample for _ in range(lax.axis_size(('row', 'co...]
    while x63 -> x70, local copies, waits for them, and re-layouts: 12.5 us -> 27.6 us
    all_to_all x0 -> x7, other arithmetic: none -> 13 us  [part_targets(): lax.all_to_all(jnp.stack([sample for _ in range(lax.axis_size(('row', 'co...]
  transfers between devices with their start and end apart: 7 -> 14, of which waited for: 7 -> 14; matrix products, arithmetic and copies ran while one was open for 0% -> 1% of each run, Pallas kernels for 0% -> 0%
where the time goes in v1:
time: 727 us; the launch traced here: 725 us
  blocking collectives  409 us (56%)
  waiting for transfers between devices  179 us (25%)
  starting transfers between devices  52.1 us (7%)
  local copies, waits for them, and re-layouts  47.7 us (7%)
  other arithmetic  24.3 us (3%)
  matrix products  12.1 us (2%)
    all_gather x7, blocking collectives, one_level(): lax.all_gather(resid, ('row', 'col'), axis=1, tiled=True)  358 us
    all_to_all x7, waiting for transfers between devices, part_targets(): lax.all_to_all(jnp.stack([sample for _ in range(lax.axis_size(('row', 'co...  119 us
    ppermute x7, waiting for transfers between devices, passed_along(): return lax.ppermute(block, axis, route)  60.1 us
    all_gather x1, blocking collectives, shards(): lax.all_gather(resid, ('row', 'col'), axis=1, tiled=True)  50.4 us
    all_to_all x7, starting transfers between devices, part_targets(): lax.all_to_all(jnp.stack([sample for _ in range(lax.axis_size(('row', 'co...  38.2 us
    while x70, local copies, waits for them, and re-layouts  27.6 us
  transfers between devices with their start and end apart: 14, of which 14 were waited for; matrix products, arithmetic and copies ran while one was open for 1% of the time, Pallas kernels for 0%

profile of v1, /device:TPU:33, one launch (start us, length us, event | category | flops | bytes accessed | tf_op | source)
XLA Modules:
  0.0 725.3 jit_solution(15725340925829995400)
XLA Ops:
  1.5 669.2 %while.16 = (s32[]{:T(128)}, f32[32,512]{0,1:T(8,128)S(1)}, f32[32,64]{1,0:T(8,128)S(1)}, s32[32]{0:T(128)S(1)}, f32[32,64]{0,1:T(8,128)S(1)}, /*index=5*/f32[64...) while((s32[]{:T(128)}, f32[32,512]{0,1:T(8,128)S(1)}, ...), condition=%wide.region_2.3_spmd.clone, body=%wide.region_0.2_spmd.clone.sunk | while | flops 151003264 | bytes 19505948 | solution.py:69
  1.8 57.0 %all-gather.4 = f32[64,64,32]{1,2,0:T(8,128)S(1)} all-gather(f32[1,64,32]{1,2,0:T(8,128)S(1)} %subtract_bitcast_fusion.2), channel_id=1, replica_groups=mesh['sep'=8,'row'=8,'col'=8] {'row','col'}, dimensions={0}, use_global_device_ids=true | all-gather | bytes 532480 | tf_op jit(solution)/shard_map/while/body/eval_jaxpr/all_gather | solution.py:60
  63.2 5.6 all-to-all-start
  69.4 17.0 %all-to-all-done = f32[64,1,2048]{2,1,0:T(1,128)S(1)} async-done(((f32[64,1,2048]{2,1,0:T(1,128)}), f32[64,1,2048]{2,1,0:T(1,128)S(1)}, u32[]{:S(2)}, u32[]{:S(2)}) %all-to-all-start) | async-done | bytes 524320 | tf_op jit(solution)/shard_map/while/body/eval_jaxpr/all_to_all | solution.py:10
  94.7 8.3 %collective-permute-done = f32[32,512]{0,1:T(8,128)S(1)} collective-permute-done((f32[32,512]{0,1:T(8,128)S(1)}, f32[32,512]{0,1:T(8,128)S(1)}, u32[]{:S(2)}, u32[]{:S(2)}) %collective-permute-start) | collective-permute-done | bytes 65568 | tf_op jit(solution)/shard_map/while/body/eval_jaxpr/ppermute | solution.py:24
  103.3 50.2 %all-gather.4 = f32[64,64,32]{1,2,0:T(8,128)S(1)} all-gather(f32[1,64,32]{1,2,0:T(8,128)S(1)} %subtract_bitcast_fusion.2), channel_id=1, replica_groups=mesh['sep'=8,'row'=8,'col'=8] {'row','col'}, dimensions={0}, use_global_device_ids=true | all-gather | bytes 532480 | tf_op jit(solution)/shard_map/while/body/eval_jaxpr/all_gather | solution.py:60
  164.0 17.0 %all-to-all-done = f32[64,1,2048]{2,1,0:T(1,128)S(1)} async-done(((f32[64,1,2048]{2,1,0:T(1,128)}), f32[64,1,2048]{2,1,0:T(1,128)S(1)}, u32[]{:S(2)}, u32[]{:S(2)}) %all-to-all-start) | async-done | bytes 524320 | tf_op jit(solution)/shard_map/while/body/eval_jaxpr/all_to_all | solution.py:10
  189.0 8.6 %collective-permute-done = f32[32,512]{0,1:T(8,128)S(1)} collective-permute-done((f32[32,512]{0,1:T(8,128)S(1)}, f32[32,512]{0,1:T(8,128)S(1)}, u32[]{:S(2)}, u32[]{:S(2)}) %collective-permute-start) | collective-permute-done | bytes 65568 | tf_op jit(solution)/shard_map/while/body/eval_jaxpr/ppermute | solution.py:24
  197.9 50.2 %all-gather.4 = f32[64,64,32]{1,2,0:T(8,128)S(1)} all-gather(f32[1,64,32]{1,2,0:T(8,128)S(1)} %subtract_bitcast_fusion.2), channel_id=1, replica_groups=mesh['sep'=8,'row'=8,'col'=8] {'row','col'}, dimensions={0}, use_global_device_ids=true | all-gather | bytes 532480 | tf_op jit(solution)/shard_map/while/body/eval_jaxpr/all_gather | solution.py:60
  258.7 17.0 %all-to-all-done = f32[64,1,2048]{2,1,0:T(1,128)S(1)} async-done(((f32[64,1,2048]{2,1,0:T(1,128)}), f32[64,1,2048]{2,1,0:T(1,128)S(1)}, u32[]{:S(2)}, u32[]{:S(2)}) %all-to-all-start) | async-done | bytes 524320 | tf_op jit(solution)/shard_map/while/body/eval_jaxpr/all_to_all | solution.py:10
  283.6 8.6 %collective-permute-done = f32[32,512]{0,1:T(8,128)S(1)} collective-permute-done((f32[32,512]{0,1:T(8,128)S(1)}, f32[32,512]{0,1:T(8,128)S(1)}, u32[]{:S(2)}, u32[]{:S(2)}) %collective-permute-start) | collective-permute-done | bytes 65568 | tf_op jit(solution)/shard_map/while/body/eval_jaxpr/ppermute | solution.py:24
  292.5 50.2 %all-gather.4 = f32[64,64,32]{1,2,0:T(8,128)S(1)} all-gather(f32[1,64,32]{1,2,0:T(8,128)S(1)} %subtract_bitcast_fusion.2), channel_id=1, replica_groups=mesh['sep'=8,'row'=8,'col'=8] {'row','col'}, dimensions={0}, use_global_device_ids=true | all-gather | bytes 532480 | tf_op jit(solution)/shard_map/while/body/eval_jaxpr/all_gather | solution.py:60
  353.3 17.0 %all-to-all-done = f32[64,1,2048]{2,1,0:T(1,128)S(1)} async-done(((f32[64,1,2048]{2,1,0:T(1,128)}), f32[64,1,2048]{2,1,0:T(1,128)S(1)}, u32[]{:S(2)}, u32[]{:S(2)}) %all-to-all-start) | async-done | bytes 524320 | tf_op jit(solution)/shard_map/while/body/eval_jaxpr/all_to_all | solution.py:10
  378.2 8.6 %collective-permute-done = f32[32,512]{0,1:T(8,128)S(1)} collective-permute-done((f32[32,512]{0,1:T(8,128)S(1)}, f32[32,512]{0,1:T(8,128)S(1)}, u32[]{:S(2)}, u32[]{:S(2)}) %collective-permute-start) | collective-permute-done | bytes 65568 | tf_op jit(solution)/shard_map/while/body/eval_jaxpr/ppermute | solution.py:24
  387.1 50.2 %all-gather.4 = f32[64,64,32]{1,2,0:T(8,128)S(1)} all-gather(f32[1,64,32]{1,2,0:T(8,128)S(1)} %subtract_bitcast_fusion.2), channel_id=1, replica_groups=mesh['sep'=8,'row'=8,'col'=8] {'row','col'}, dimensions={0}, use_global_device_ids=true | all-gather | bytes 532480 | tf_op jit(solution)/shard_map/while/body/eval_jaxpr/all_gather | solution.py:60
  447.9 17.0 %all-to-all-done = f32[64,1,2048]{2,1,0:T(1,128)S(1)} async-done(((f32[64,1,2048]{2,1,0:T(1,128)}), f32[64,1,2048]{2,1,0:T(1,128)S(1)}, u32[]{:S(2)}, u32[]{:S(2)}) %all-to-all-start) | async-done | bytes 524320 | tf_op jit(solution)/shard_map/while/body/eval_jaxpr/all_to_all | solution.py:10
  472.8 8.6 %collective-permute-done = f32[32,512]{0,1:T(8,128)S(1)} collective-permute-done((f32[32,512]{0,1:T(8,128)S(1)}, f32[32,512]{0,1:T(8,128)S(1)}, u32[]{:S(2)}, u32[]{:S(2)}) %collective-permute-start) | collective-permute-done | bytes 65568 | tf_op jit(solution)/shard_map/while/body/eval_jaxpr/ppermute | solution.py:24
  481.7 50.2 %all-gather.4 = f32[64,64,32]{1,2,0:T(8,128)S(1)} all-gather(f32[1,64,32]{1,2,0:T(8,128)S(1)} %subtract_bitcast_fusion.2), channel_id=1, replica_groups=mesh['sep'=8,'row'=8,'col'=8] {'row','col'}, dimensions={0}, use_global_device_ids=true | all-gather | bytes 532480 | tf_op jit(solution)/shard_map/while/body/eval_jaxpr/all_gather | solution.py:60
  542.5 17.0 %all-to-all-done = f32[64,1,2048]{2,1,0:T(1,128)S(1)} async-done(((f32[64,1,2048]{2,1,0:T(1,128)}), f32[64,1,2048]{2,1,0:T(1,128)S(1)}, u32[]{:S(2)}, u32[]{:S(2)}) %all-to-all-start) | async-done | bytes 524320 | tf_op jit(solution)/shard_map/while/body/eval_jaxpr/all_to_all | solution.py:10
  567.4 8.6 %collective-permute-done = f32[32,512]{0,1:T(8,128)S(1)} collective-permute-done((f32[32,512]{0,1:T(8,128)S(1)}, f32[32,512]{0,1:T(8,128)S(1)}, u32[]{:S(2)}, u32[]{:S(2)}) %collective-permute-start) | collective-permute-done | bytes 65568 | tf_op jit(solution)/shard_map/while/body/eval_jaxpr/ppermute | solution.py:24
  576.3 50.2 %all-gather.4 = f32[64,64,32]{1,2,0:T(8,128)S(1)} all-gather(f32[1,64,32]{1,2,0:T(8,128)S(1)} %subtract_bitcast_fusion.2), channel_id=1, replica_groups=mesh['sep'=8,'row'=8,'col'=8] {'row','col'}, dimensions={0}, use_global_device_ids=true | all-gather | bytes 532480 | tf_op jit(solution)/shard_map/while/body/eval_jaxpr/all_gather | solution.py:60
  637.1 17.0 %all-to-all-done = f32[64,1,2048]{2,1,0:T(1,128)S(1)} async-done(((f32[64,1,2048]{2,1,0:T(1,128)}), f32[64,1,2048]{2,1,0:T(1,128)S(1)}, u32[]{:S(2)}, u32[]{:S(2)}) %all-to-all-start) | async-done | bytes 524320 | tf_op jit(solution)/shard_map/while/body/eval_jaxpr/all_to_all | solution.py:10
  662.0 8.6 %collective-permute-done = f32[32,512]{0,1:T(8,128)S(1)} collective-permute-done((f32[32,512]{0,1:T(8,128)S(1)}, f32[32,512]{0,1:T(8,128)S(1)}, u32[]{:S(2)}, u32[]{:S(2)}) %collective-permute-start) | collective-permute-done | bytes 65568 | tf_op jit(solution)/shard_map/while/body/eval_jaxpr/ppermute | solution.py:24
  671.5 50.4 %all-gather.1 = f32[64,64,32]{1,2,0:T(8,128)S(1)} all-gather(f32[1,64,32]{1,2,0:T(8,128)S(1)} %fusion.4), channel_id=1, replica_groups=mesh['sep'=8,'row'=8,'col'=8] {'row','col'}, dimensions={0}, use_global_device_ids=true | all-gather | bytes 532480 | tf_op jit(solution)/shard_map/all_gather | solution.py:72
  (189 shorter events, 130.6 us)
Async XLA Ops:
  59.4 1.2 copy-start
  63.2 23.3 %all-to-all-start = ((f32[64,1,2048]{2,1,0:T(1,128)}), f32[64,1,2048]{2,1,0:T(1,128)S(1)}, u32[]{:S(2)}, u32[]{:S(2)}) async-start(f32[64,1,2048]{2,1,0:T(1,128)} %reshape.73), calls=%async_computation | async-start | bytes 1048576 | tf_op jit(solution)/shard_map/while/body/eval_jaxpr/all_to_all | solution.py:10
  89.9 1.0 copy-start.2
  92.4 10.6 %collective-permute-start = (f32[32,512]{0,1:T(8,128)S(1)}, f32[32,512]{0,1:T(8,128)S(1)}, u32[]{:S(2)}, u32[]{:S(2)}) collective-permute-start(f32[32,512]{0,1:T(8,128)S(1)} %scatter_fusion), channel_id=1, source_target_pairs={{0,64},{64,128},{128,192},{192,256},{256,320},{320,384},{384,448},... | collective-permute-start | bytes 196616 | tf_op jit(solution)/shard_map/while/body/eval_jaxpr/ppermute | solution.py:24
  154.1 1.2 copy-start
  157.9 23.1 %all-to-all-start = ((f32[64,1,2048]{2,1,0:T(1,128)}), f32[64,1,2048]{2,1,0:T(1,128)S(1)}, u32[]{:S(2)}, u32[]{:S(2)}) async-start(f32[64,1,2048]{2,1,0:T(1,128)} %reshape.73), calls=%async_computation | async-start | bytes 1048576 | tf_op jit(solution)/shard_map/while/body/eval_jaxpr/all_to_all | solution.py:10
  184.5 1.0 copy-start.2
  187.0 10.6 %collective-permute-start = (f32[32,512]{0,1:T(8,128)S(1)}, f32[32,512]{0,1:T(8,128)S(1)}, u32[]{:S(2)}, u32[]{:S(2)}) collective-permute-start(f32[32,512]{0,1:T(8,128)S(1)} %scatter_fusion), channel_id=1, source_target_pairs={{0,64},{64,128},{128,192},{192,256},{256,320},{320,384},{384,448},... | collective-permute-start | bytes 196616 | tf_op jit(solution)/shard_map/while/body/eval_jaxpr/ppermute | solution.py:24
  248.8 1.2 copy-start
  252.5 23.1 %all-to-all-start = ((f32[64,1,2048]{2,1,0:T(1,128)}), f32[64,1,2048]{2,1,0:T(1,128)S(1)}, u32[]{:S(2)}, u32[]{:S(2)}) async-start(f32[64,1,2048]{2,1,0:T(1,128)} %reshape.73), calls=%async_computation | async-start | bytes 1048576 | tf_op jit(solution)/shard_map/while/body/eval_jaxpr/all_to_all | solution.py:10
  281.6 10.6 %collective-permute-start = (f32[32,512]{0,1:T(8,128)S(1)}, f32[32,512]{0,1:T(8,128)S(1)}, u32[]{:S(2)}, u32[]{:S(2)}) collective-permute-start(f32[32,512]{0,1:T(8,128)S(1)} %scatter_fusion), channel_id=1, source_target_pairs={{0,64},{64,128},{128,192},{192,256},{256,320},{320,384},{384,448},... | collective-permute-start | bytes 196616 | tf_op jit(solution)/shard_map/while/body/eval_jaxpr/ppermute | solution.py:24
  343.4 1.2 copy-start
  347.1 23.1 %all-to-all-start = ((f32[64,1,2048]{2,1,0:T(1,128)}), f32[64,1,2048]{2,1,0:T(1,128)S(1)}, u32[]{:S(2)}, u32[]{:S(2)}) async-start(f32[64,1,2048]{2,1,0:T(1,128)} %reshape.73), calls=%async_computation | async-start | bytes 1048576 | tf_op jit(solution)/shard_map/while/body/eval_jaxpr/all_to_all | solution.py:10
  376.2 10.6 %collective-permute-start = (f32[32,512]{0,1:T(8,128)S(1)}, f32[32,512]{0,1:T(8,128)S(1)}, u32[]{:S(2)}, u32[]{:S(2)}) collective-permute-start(f32[32,512]{0,1:T(8,128)S(1)} %scatter_fusion), channel_id=1, source_target_pairs={{0,64},{64,128},{128,192},{192,256},{256,320},{320,384},{384,448},... | collective-permute-start | bytes 196616 | tf_op jit(solution)/shard_map/while/body/eval_jaxpr/ppermute | solution.py:24
  438.0 1.2 copy-start
  441.7 23.1 %all-to-all-start = ((f32[64,1,2048]{2,1,0:T(1,128)}), f32[64,1,2048]{2,1,0:T(1,128)S(1)}, u32[]{:S(2)}, u32[]{:S(2)}) async-start(f32[64,1,2048]{2,1,0:T(1,128)} %reshape.73), calls=%async_computation | async-start | bytes 1048576 | tf_op jit(solution)/shard_map/while/body/eval_jaxpr/all_to_all | solution.py:10
  470.9 10.6 %collective-permute-start = (f32[32,512]{0,1:T(8,128)S(1)}, f32[32,512]{0,1:T(8,128)S(1)}, u32[]{:S(2)}, u32[]{:S(2)}) collective-permute-start(f32[32,512]{0,1:T(8,128)S(1)} %scatter_fusion), channel_id=1, source_target_pairs={{0,64},{64,128},{128,192},{192,256},{256,320},{320,384},{384,448},... | collective-permute-start | bytes 196616 | tf_op jit(solution)/shard_map/while/body/eval_jaxpr/ppermute | solution.py:24
  532.6 1.2 copy-start
  536.4 23.1 %all-to-all-start = ((f32[64,1,2048]{2,1,0:T(1,128)}), f32[64,1,2048]{2,1,0:T(1,128)S(1)}, u32[]{:S(2)}, u32[]{:S(2)}) async-start(f32[64,1,2048]{2,1,0:T(1,128)} %reshape.73), calls=%async_computation | async-start | bytes 1048576 | tf_op jit(solution)/shard_map/while/body/eval_jaxpr/all_to_all | solution.py:10
  565.5 10.6 %collective-permute-start = (f32[32,512]{0,1:T(8,128)S(1)}, f32[32,512]{0,1:T(8,128)S(1)}, u32[]{:S(2)}, u32[]{:S(2)}) collective-permute-start(f32[32,512]{0,1:T(8,128)S(1)} %scatter_fusion), channel_id=1, source_target_pairs={{0,64},{64,128},{128,192},{192,256},{256,320},{320,384},{384,448},... | collective-permute-start | bytes 196616 | tf_op jit(solution)/shard_map/while/body/eval_jaxpr/ppermute | solution.py:24
  627.2 1.2 copy-start
  631.0 23.1 %all-to-all-start = ((f32[64,1,2048]{2,1,0:T(1,128)}), f32[64,1,2048]{2,1,0:T(1,128)S(1)}, u32[]{:S(2)}, u32[]{:S(2)}) async-start(f32[64,1,2048]{2,1,0:T(1,128)} %reshape.73), calls=%async_computation | async-start | bytes 1048576 | tf_op jit(solution)/shard_map/while/body/eval_jaxpr/all_to_all | solution.py:10
  660.1 10.6 %collective-permute-start = (f32[32,512]{0,1:T(8,128)S(1)}, f32[32,512]{0,1:T(8,128)S(1)}, u32[]{:S(2)}, u32[]{:S(2)}) collective-permute-start(f32[32,512]{0,1:T(8,128)S(1)} %scatter_fusion), channel_id=1, source_target_pairs={{0,64},{64,128},{128,192},{192,256},{256,320},{320,384},{384,448},... | collective-permute-start | bytes 196616 | tf_op jit(solution)/shard_map/while/body/eval_jaxpr/ppermute | solution.py:24
  722.5 1.2 copy-start.1
  (7 other events, 6.6 us)
